TPU v7x, 512 devices: a whole 4x8x8 slice. The times are simulated.
512 devices in a mesh: req: 64 (over x, y, core), tp: 8 (over z).
Axes of the slice: x: 4, y: 8, z: 8, core: 2. Of those that a mesh axis runs over, the one named last changes fastest.
Arguments:
- vit_context: bfloat16 [32768, 4096], P('req', 'tp'), may hold values from -6 to 6
- vision_residual: bfloat16 [32768, 4096], P('req', 'tp'), may hold values from -75 to 75
- out_weight: bfloat16 [4096, 4096], P('tp', 'req'), may hold values from -0.09375 to 0.09375
- layer_scale: float32 [4096], P('tp'), may hold values from 0.2 to 2
- prompt: bfloat16 [64, 256, 4096], P('req', None, 'tp'), may hold values from -75 to 75
- prompt_len: int32 [64], P('req'), may hold values from 128 to 256
- image_at: int32 [64], P('req'), may hold values from 0 to 128
- grid_sizes: int32 [128, 2], replicated, may hold values from 7 to 8, as said below
- image_owner: int32 [128], replicated, may hold values from 0 to 63, as said below
- norm_gain: float32 [4096], replicated, may hold values from 0.5 to 1.5
- qkv_weight: bfloat16 [4096, 6144], P('req', 'tp'), may hold values from -0.09375 to 0.09375
Outputs:
- qkv: bfloat16 [24576, 6144], P('req', 'tp')
Inputs may be any that keep to these rules, and one draw needn't show every extreme that they name: `image_owner`: each request owns exactly 2 images. `grid_sizes`: each side is 7 or 8; in every draw the images of some request are all 8 by 8, so that request has exactly 128 merged rows.
All inputs are finite; a program needn't handle non-finite values.
Results may differ from a plain program's by a relative error of at most 0.008.
Values may be sent and summed in bfloat16 or wider, within the bound.
No kernel may reach another device: no remote copies, remote signals or barrier semaphores. Data moves between devices by JAX's collectives and lax.ppermute only.
A program may use at most 64 MiB of HBM per device.

v0:
```python
import jax
import jax.numpy as jnp
from jax import lax
from jax.sharding import PartitionSpec as P

HEAD = 128
GROUP = 4
IMG_MAX = 128


def request_plan(grid_sizes, image_owner, requests):
    image_rows = grid_sizes[:, 0] * grid_sizes[:, 1]
    member = (image_owner[:, None] == jnp.arange(requests, dtype=jnp.int32)[None, :]).astype(
        jnp.int32
    )
    counts = jnp.sum(image_rows[:, None] * member, axis=0)
    starts = jnp.cumsum(counts) - counts
    return (counts, starts)


def rope_tables(count):
    half_size = HEAD // 2
    exponent = jnp.arange(half_size, dtype=jnp.float32) * (2.0 / HEAD)
    frequency = jnp.exp(-exponent * jnp.log(jnp.float32(500000.0)))
    angles = jnp.arange(count, dtype=jnp.float32)[:, None] * frequency[None, :]
    return (jnp.cos(angles), jnp.sin(angles))


def apply_rope(projected, cosine_table, sine_table):
    seq_rows = projected.shape[0]
    head_blocks = projected.reshape(seq_rows, -1, GROUP + 2, HEAD)
    turning = head_blocks[:, :, : GROUP + 1, :]
    first_half = turning[..., : HEAD // 2]
    second_half = turning[..., HEAD // 2 :]
    cosine_wide = cosine_table[:, None, None, :]
    sine_wide = sine_table[:, None, None, :]
    turned = jnp.concatenate(
        [
            first_half * cosine_wide - second_half * sine_wide,
            second_half * cosine_wide + first_half * sine_wide,
        ],
        axis=-1,
    )
    head_blocks = jnp.concatenate([turned, head_blocks[:, :, GROUP + 1 :, :]], axis=2)
    return head_blocks.reshape(seq_rows, -1)


def normalize(embedded, norm_gain):
    values = embedded.astype(jnp.float32)
    mean_square = jnp.mean(values * values, axis=-1, keepdims=True)
    return (values * lax.rsqrt(mean_square + 1e-05) * norm_gain[None, :]).astype(jnp.bfloat16)


def shards(
    vit_context,
    vision_residual,
    out_weight,
    layer_scale,
    prompt,
    prompt_len,
    image_at,
    grid_sizes,
    image_owner,
    norm_gain,
    qkv_weight,
):
    requests = lax.axis_size("req")
    device_index = lax.axis_index("req")
    feature_width = vit_context.shape[1]
    merged_context = jnp.mean(
        vit_context.astype(jnp.float32).reshape(-1, 4, feature_width), axis=1
    ).astype(jnp.bfloat16)
    merged_residual = jnp.mean(
        vision_residual.astype(jnp.float32).reshape(-1, 4, feature_width), axis=1
    )
    partial_value = jnp.dot(
        merged_context,
        lax.all_gather(out_weight, "req", axis=1, tiled=True),
        preferred_element_type=jnp.float32,
    )
    summed = lax.psum(partial_value.astype(jnp.bfloat16), "tp").astype(jnp.float32)
    own_share = lax.dynamic_slice_in_dim(
        summed, lax.axis_index("tp") * feature_width, feature_width, 1
    )
    merged = (merged_residual + layer_scale[None, :] * own_share).astype(jnp.bfloat16)
    merged_count = merged.shape[0]
    counts, starts = request_plan(grid_sizes, image_owner, requests)
    request_ends = starts + counts
    capacity = (IMG_MAX + requests - 1) // requests
    request_ids = jnp.arange(requests, dtype=jnp.int32)
    group_index = jnp.arange(merged_count, dtype=jnp.int32) * requests + device_index
    destination = jnp.sum((request_ends[None, :] <= group_index[:, None]).astype(jnp.int32), axis=1)
    owned_start = jnp.sum(
        jnp.where(destination[:, None] == request_ids[None, :], starts[None, :], 0), axis=1
    )
    target = destination * capacity + (group_index - owned_start) // requests
    usable = destination < requests
    send_slots = jnp.arange(requests * capacity, dtype=jnp.int32)
    placing = ((send_slots[:, None] == target[None, :]) & usable[None, :]).astype(jnp.bfloat16)
    outgoing = jnp.dot(placing, merged, preferred_element_type=jnp.float32).astype(jnp.bfloat16)
    arrived = lax.all_to_all(
        outgoing.reshape(requests, capacity, feature_width),
        "req",
        split_axis=0,
        concat_axis=0,
        tiled=True,
    )
    arrived = arrived.reshape(requests * capacity, feature_width)
    own_request = request_ids == device_index
    own_count = jnp.sum(jnp.where(own_request, counts, 0))
    own_start = jnp.sum(jnp.where(own_request, starts, 0))
    image_from = image_at[0]
    prompt_count = prompt_len[0]
    seq_slots = prompt.shape[1] + IMG_MAX
    slot_index = jnp.arange(seq_slots, dtype=jnp.int32)
    image_row = slot_index - image_from
    in_image = (image_row >= 0) & (image_row < own_count)
    is_live = slot_index < prompt_count + own_count
    from_prompt = is_live & jnp.logical_not(in_image)
    flat_index = (own_start + image_row) % requests * capacity + image_row // requests
    image_pick = ((flat_index[:, None] == send_slots[None, :]) & in_image[:, None]).astype(
        jnp.bfloat16
    )
    prompt_row = jnp.where(slot_index < image_from, slot_index, slot_index - own_count)
    prompt_ids = jnp.arange(prompt.shape[1], dtype=jnp.int32)
    prompt_pick = ((prompt_row[:, None] == prompt_ids[None, :]) & from_prompt[:, None]).astype(
        jnp.bfloat16
    )
    embedded = (
        jnp.dot(image_pick, arrived, preferred_element_type=jnp.float32)
        + jnp.dot(prompt_pick, prompt[0], preferred_element_type=jnp.float32)
    ).astype(jnp.bfloat16)
    gathered = lax.all_gather(embedded, "tp", axis=1, tiled=True)
    normed = normalize(gathered, norm_gain)
    projected = jnp.dot(
        normed,
        lax.all_gather(qkv_weight, "req", axis=0, tiled=True),
        preferred_element_type=jnp.float32,
    )
    cosine_table, sine_table = rope_tables(seq_slots)
    return apply_rope(projected, cosine_table, sine_table).astype(jnp.bfloat16)


def solution(mesh):
    in_specs = (
        P("req", "tp"),
        P("req", "tp"),
        P("tp", "req"),
        P("tp"),
        P("req", None, "tp"),
        P("req"),
        P("req"),
        P(),
        P(),
        P(),
        P("req", "tp"),
    )
    out_specs = P("req", "tp")
    return jax.shard_map(shards, mesh=mesh, in_specs=in_specs, out_specs=out_specs, check_vma=False)
```

profile of v0, /device:TPU:1, one launch (start us, length us, event | category | flops | bytes accessed | tf_op | source)
XLA Modules:
  0.0 352.9 jit_solution(7770393168710454331)
XLA Ops:
  6.5 0.7 all-gather.4.cloned.1.call-update
  7.3 1.4 reshape.205
  8.7 0.6 reduce_sum.78
  9.3 0.8 multiply_bitcast_fusion
  10.1 91.0 %all-gather.4.cloned.1.call-done = bf16[512,4096]{0,1:T(8,128)(2,1)} async-done(((bf16[512,64]{0,1:T(8,128)(2,1)}), bf16[512,4096]{0,1:T(8,128)(2,1)}) %all-gather.4.cloned.1.call-update) | async-done | bytes 4194320 | tf_op jit(solution)/shard_map/all_gather | solution.py:78
  101.1 4.6 %convolution_convert_fusion = bf16[128,4096]{1,0:T(8,128)(2,1)} fusion(bf16[512,4096]{0,1:T(8,128)(2,1)} %all-gather.4.cloned.1.call-done, f32[128,512]{1,0:T(8,128)S(1)} %reduce_sum.78), kind=kOutput, calls=%fused_computation.5 | convolution fusion | flops 537526272 | bytes 5505024 | tf_op jit(solution)/shard_map/dot_general | solution.py:76
  105.7 0.1 select_reduce_fusion.1
  105.8 0.1 copy.16
  105.9 0.1 reduce-window.7
  106.0 0.1 reduce
  106.2 0.3 reshape.203
  106.5 0.6 reduce_sum.77
  107.2 0.1 convert_reduce_fusion
  107.3 0.7 fusion.38
  108.0 0.1 select_reduce_fusion
  108.1 73.3 %all-reduce.2.cloned.1.call-done = bf16[128,4096]{1,0:T(8,128)(2,1)} async-done(((bf16[128,4096]{1,0:T(8,128)(2,1)}), bf16[128,4096]{1,0:T(8,128)(2,1)}) %all-reduce.2.cloned.1.call-update) | async-done | bytes 1048592 | tf_op jit(solution)/shard_map/psum | solution.py:81
  181.4 1.1 convolution_convert_fusion.1
  182.5 0.7 reshape.199
  183.3 14.2 %all-to-all-start = ((bf16[64,2,512]{2,1,0:T(2,128)(2,1)}), bf16[64,2,512]{2,1,0:T(2,128)(2,1)S(1)}, u32[]{:S(2)}, u32[]{:S(2)}) async-start(bf16[64,2,512]{2,1,0:T(2,128)(2,1)} %reshape.199), calls=%async_computation | async-start | bytes 262144 | tf_op jit(solution)/shard_map/all_to_all | solution.py:101
  199.3 0.6 fusion.37
  199.9 1.3 fusion.30
  201.2 6.6 %all-to-all-done = bf16[64,2,512]{2,1,0:T(2,128)(2,1)S(1)} async-done(((bf16[64,2,512]{2,1,0:T(2,128)(2,1)}), bf16[64,2,512]{2,1,0:T(2,128)(2,1)S(1)}, u32[]{:S(2)}, u32[]{:S(2)}) %all-to-all-start) | async-done | bytes 131104 | tf_op jit(solution)/shard_map/all_to_all | solution.py:101
  207.9 0.3 fusion.14
  208.2 1.1 fusion.7
  209.3 0.5 all-gather.8.cloned.1.call-update
  209.9 0.4 fusion.21
  210.3 40.0 %all-gather.6.cloned.1.call-done = bf16[384,4096]{1,0:T(8,128)(2,1)} async-done(((bf16[384,512]{1,0:T(8,128)(2,1)}), bf16[384,4096]{1,0:T(8,128)(2,1)}) %all-gather.6.cloned.1.call-update) | async-done | bytes 3145744 | tf_op jit(solution)/shard_map/all_gather | solution.py:133
  250.3 2.6 fusion
  252.9 85.4 %all-gather.8.cloned.1.call-done = bf16[4096,768]{1,0:T(8,128)(2,1)} async-done(((bf16[64,768]{1,0:T(8,128)(2,1)}), bf16[4096,768]{1,0:T(8,128)(2,1)}) %all-gather.8.cloned.1.call-update) | async-done | bytes 6291472 | tf_op jit(solution)/shard_map/all_gather | solution.py:137
  338.3 6.7 %fusion.3 = f32[384,768]{0,1:T(8,128)S(1)} fusion(bf16[4096,768]{1,0:T(8,128)(2,1)} %all-gather.8.cloned.1.call-done, bf16[384,4096]{1,0:T(8,128)(2,1)} %all-gather.6.cloned.1.call-done, f32[4096]{0:T(1024)S(1)} %copy-done.3, f32[384]{0:T(512)S(1)} %add_rsqrt_fusion), kind=kOutput, calls=%fused_computation.6 | convolution fusion | flops 2422210560 | bytes 10634752 | tf_op jit(solution)/shard_map/dot_general | solution.py:135
  345.0 0.1 subtract_convert_fusion
  345.2 1.1 copy.18
  (24 shorter events, 0.4 us)
Async XLA Ops:
  6.5 201.7 %copy-start = (bf16[1,256,512]{2,1,0:T(8,128)(2,1)S(1)}, bf16[1,256,512]{2,1,0:T(8,128)(2,1)}, u32[]{:S(2)}) copy-start(bf16[1,256,512]{2,1,0:T(8,128)(2,1)} %param.15) | copy-start | bytes 786436
  6.5 94.5 %all-gather.4.cloned.1.call-start = ((), (), s32[]{:S(2)}) async-start(), calls=%async_computation.1 | async-start | bytes 4259840 | tf_op jit(solution)/shard_map/all_gather | solution.py:78
  7.3 174.2 %all-reduce.2.cloned.1.call-start = ((), (), s32[]{:S(2)}) async-start(), calls=%async_computation.2 | async-start | bytes 2097152 | tf_op jit(solution)/shard_map/psum | solution.py:81
  8.7 97.0 %copy-start.4 = (s32[128]{0:T(128)S(1)}, s32[128]{0:T(128)}, u32[]{:S(2)}) copy-start(s32[128]{0:T(128)} %param.19) | copy-start | bytes 1540
  8.7 97.5 %copy-start.1 = (bf16[512,512]{1,0:T(8,128)(2,1)S(1)}, bf16[512,512]{1,0:T(8,128)(2,1)}, u32[]{:S(2)}) copy-start(bf16[512,512]{1,0:T(8,128)(2,1)} %param.12) | copy-start | bytes 1572868
  10.1 171.3 %copy-start.2 = (f32[512]{0:T(512)S(1)}, f32[512]{0:T(512)}, u32[]{:S(2)}) copy-start(f32[512]{0:T(512)} %param.14) | copy-start | bytes 6148
  106.5 231.8 %copy-start.3 = (f32[4096]{0:T(1024)S(1)}, f32[4096]{0:T(1024)}, u32[]{:S(2)}) copy-start(f32[4096]{0:T(1024)} %param.20) | copy-start | bytes 49156
  183.3 24.5 %all-to-all-start = ((bf16[64,2,512]{2,1,0:T(2,128)(2,1)}), bf16[64,2,512]{2,1,0:T(2,128)(2,1)S(1)}, u32[]{:S(2)}, u32[]{:S(2)}) async-start(bf16[64,2,512]{2,1,0:T(2,128)(2,1)} %reshape.199), calls=%async_computation | async-start | bytes 262144 | tf_op jit(solution)/shard_map/all_to_all | solution.py:101
  197.4 52.9 %all-gather.6.cloned.1.call-start = ((), (), s32[]{:S(2)}) async-start(), calls=%async_computation.3 | async-start | bytes 3538944 | tf_op jit(solution)/shard_map/all_gather | solution.py:133
  209.3 129.0 %all-gather.8.cloned.1.call-start = ((), (), s32[]{:S(2)}) async-start(), calls=%async_computation.4 | async-start | bytes 6389760 | tf_op jit(solution)/shard_map/all_gather | solution.py:137
Sparse Core Ops, SparseCore 0:
  10.7 90.2 all-gather.3
  105.8 75.5 all-reduce.1
  209.4 40.8 all-gather.5
  253.5 84.7 all-gather.7
where the time goes:
time: 353 us
  waiting for transfers between devices  298 us (84%)
  between operations  15.2 us (4%)
  starting transfers between devices  14.3 us (4%)
  matrix products  13.8 us (4%)
  other arithmetic  8.27 us (2%)
  local copies, waits for them, and re-layouts  3.69 us (1%)
    all_gather x1, waiting for transfers between devices, shards(): lax.all_gather(out_weight, 'req', axis=1, tiled=True)  91 us
    all_gather x1, waiting for transfers between devices, shards(): lax.all_gather(qkv_weight, 'req', axis=0, tiled=True)  85.4 us
    psum x1, waiting for transfers between devices, shards(): lax.psum(partial_value.astype(jnp.bfloat16), 'tp').astype(jnp.float32)  73.3 us
    all_gather x1, waiting for transfers between devices, shards(): gathered = lax.all_gather(embedded, 'tp', axis=1, tiled=True)  40 us
    all_to_all x1, starting transfers between devices, shards(): lax.all_to_all(outgoing.reshape(requests, capacity, feature_width), 'req'...  14.2 us
  transfers between devices with their start and end apart: 5, of which 5 were waited for; matrix products, arithmetic and copies ran while one was open for 3% of the time, Pallas kernels for 0%

commit v1 on v0

--- a/solution.py
+++ b/solution.py
@@ -78,7 +78,9 @@
         lax.all_gather(out_weight, "req", axis=1, tiled=True),
         preferred_element_type=jnp.float32,
     )
-    summed = lax.psum(partial_value.astype(jnp.bfloat16), "tp").astype(jnp.float32)
+    summed = jnp.sum(lax.all_gather(partial_value.astype(jnp.bfloat16), "tp"), axis=0).astype(
+        jnp.float32
+    )
     own_share = lax.dynamic_slice_in_dim(
         summed, lax.axis_index("tp") * feature_width, feature_width, 1
     )

time: 353 us -> 373 us (1.057)
  waiting for transfers between devices: 298 us -> 317 us
  other arithmetic: 8.27 us -> 12.6 us
  starting transfers between devices: 14.3 us -> 10.5 us
    all_gather x0 -> x1, waiting for transfers between devices: none -> 92.5 us  [shards(): lax.all_gather(partial_value.astype(jnp.bfloat16), 'tp')]
    psum x1 -> x0, waiting for transfers between devices: 73.3 us -> none  [shards(): lax.psum(partial_value.astype(jnp.bfloat16), 'tp').astype(jnp.float32)]
    reduce_sum x0 -> x1, other arithmetic: none -> 4.91 us  [shards(): jnp.sum(lax.all_gather(partial_value.astype(jnp.bfloat16), 'tp'), axis=0)]
    all_to_all x1, starting transfers between devices: 14.2 us -> 10.4 us  [shards(): lax.all_to_all(outgoing.reshape(requests, capacity, feature_width), 'req'...]
  transfers between devices with their start and end apart: 5 -> 5, of which waited for: 5 -> 5; matrix products, arithmetic and copies ran while one was open for 3% -> 2% of each run, Pallas kernels for 0% -> 0%
where the time goes in v1:
time: 373 us
  waiting for transfers between devices  317 us (85%)
  between operations  15.3 us (4%)
  matrix products  13.1 us (4%)
  other arithmetic  12.6 us (3%)
  starting transfers between devices  10.5 us (3%)
    all_gather x1, waiting for transfers between devices, shards(): lax.all_gather(partial_value.astype(jnp.bfloat16), 'tp')  92.5 us
    all_gather x1, waiting for transfers between devices, shards(): lax.all_gather(out_weight, 'req', axis=1, tiled=True)  91.7 us
    all_gather x1, waiting for transfers between devices, shards(): lax.all_gather(qkv_weight, 'req', axis=0, tiled=True)  85.4 us
    all_gather x1, waiting for transfers between devices, shards(): gathered = lax.all_gather(embedded, 'tp', axis=1, tiled=True)  40.2 us
    all_to_all x1, starting transfers between devices, shards(): lax.all_to_all(outgoing.reshape(requests, capacity, feature_width), 'req'...  10.4 us
  transfers between devices with their start and end apart: 5, of which 5 were waited for; matrix products, arithmetic and copies ran while one was open for 2% of the time, Pallas kernels for 0%

profile of v1, /device:TPU:1, one launch (start us, length us, event | category | flops | bytes accessed | tf_op | source)
XLA Modules:
  0.0 372.5 jit_solution(10457048197082466468)
XLA Ops:
  6.5 0.7 all-gather.6.cloned.1.call-update
  7.3 1.4 reshape.205
  8.7 0.6 reduce_sum.90
  9.3 91.7 %all-gather.6.cloned.1.call-done = bf16[512,4096]{0,1:T(8,128)(2,1)} async-done(((bf16[512,64]{0,1:T(8,128)(2,1)}), bf16[512,4096]{0,1:T(8,128)(2,1)}) %all-gather.6.cloned.1.call-update) | async-done | bytes 4194320 | tf_op jit(solution)/shard_map/all_gather | solution.py:78
  101.1 4.7 %convolution_convert_fusion = bf16[128,4096]{1,0:T(8,128)(2,1)} fusion(bf16[512,4096]{0,1:T(8,128)(2,1)} %all-gather.6.cloned.1.call-done, f32[128,512]{1,0:T(8,128)S(1)} %reduce_sum.90), kind=kOutput, calls=%fused_computation.5 | convolution fusion | flops 537526272 | bytes 5505024 | tf_op jit(solution)/shard_map/dot_general | solution.py:76
  105.9 0.1 select_reduce_fusion.1
  106.0 0.1 copy.16
  106.1 0.1 reduce-window.7
  106.2 0.1 reduce.1
  106.3 0.3 reshape.203
  106.6 0.6 reduce_sum.89
  107.3 0.1 convert_reduce_fusion
  107.4 0.7 fusion.38
  108.1 0.1 select_reduce_fusion
  108.2 92.5 %all-gather.12.cloned.1.call-done = bf16[1024,4096]{1,0:T(8,128)(2,1)} async-done(((bf16[128,4096]{1,0:T(8,128)(2,1)}), bf16[1024,4096]{1,0:T(8,128)(2,1)}) %all-gather.12.cloned.1.call-update) | async-done | bytes 8388624 | tf_op jit(solution)/shard_map/all_gather | solution.py:81
  200.7 4.9 %reduce_sum.91 = bf16[128,4096]{1,0:T(8,128)(2,1)S(1)} reduce(bf16[8,128,4096]{2,1,0:T(8,128)(2,1)} %bitcast.17, bf16[]{:T(256)} %constant.69.clone.1), dimensions={0}, to_apply=%region_8.9 | reduce | flops 3670016 | bytes 9437186 | tf_op jit(solution)/shard_map/reduce_sum | solution.py:81
  205.6 0.2 convolution_convert_fusion.1
  205.9 0.7 reshape.199
  206.6 10.4 %all-to-all-start = ((bf16[64,2,512]{2,1,0:T(2,128)(2,1)}), bf16[64,2,512]{2,1,0:T(2,128)(2,1)S(1)}, u32[]{:S(2)}, u32[]{:S(2)}) async-start(bf16[64,2,512]{2,1,0:T(2,128)(2,1)} %reshape.199), calls=%async_computation | async-start | bytes 262144 | tf_op jit(solution)/shard_map/all_to_all | solution.py:103
  219.0 0.7 fusion.37
  219.7 1.3 fusion.30
  221.0 6.3 %all-to-all-done = bf16[64,2,512]{2,1,0:T(2,128)(2,1)S(1)} async-done(((bf16[64,2,512]{2,1,0:T(2,128)(2,1)}), bf16[64,2,512]{2,1,0:T(2,128)(2,1)S(1)}, u32[]{:S(2)}, u32[]{:S(2)}) %all-to-all-start) | async-done | bytes 131104 | tf_op jit(solution)/shard_map/all_to_all | solution.py:103
  227.4 0.3 fusion.14
  227.7 1.1 fusion.7
  228.9 0.5 all-gather.10.cloned.1.call-update
  229.4 0.4 fusion.21
  229.8 40.2 %all-gather.8.cloned.1.call-done = bf16[384,4096]{1,0:T(8,128)(2,1)} async-done(((bf16[384,512]{1,0:T(8,128)(2,1)}), bf16[384,4096]{1,0:T(8,128)(2,1)}) %all-gather.8.cloned.1.call-update) | async-done | bytes 3145744 | tf_op jit(solution)/shard_map/all_gather | solution.py:135
  270.0 2.6 fusion
  272.6 85.4 %all-gather.10.cloned.1.call-done = bf16[4096,768]{1,0:T(8,128)(2,1)} async-done(((bf16[64,768]{1,0:T(8,128)(2,1)}), bf16[4096,768]{1,0:T(8,128)(2,1)}) %all-gather.10.cloned.1.call-update) | async-done | bytes 6291472 | tf_op jit(solution)/shard_map/all_gather | solution.py:139
  358.0 6.7 %fusion.3 = f32[384,768]{0,1:T(8,128)S(1)} fusion(bf16[4096,768]{1,0:T(8,128)(2,1)} %all-gather.10.cloned.1.call-done, bf16[384,4096]{1,0:T(8,128)(2,1)} %all-gather.8.cloned.1.call-done, f32[4096]{0:T(1024)S(1)} %copy-done.3, f32[384]{0:T(512)S(1)} %add_rsqrt_fusion), kind=kOutput, calls=%fused_computation.6 | convolution fusion | flops 2422210560 | bytes 10634752 | tf_op jit(solution)/shard_map/dot_general | solution.py:137
  364.7 0.1 subtract_convert_fusion
  364.9 1.1 copy.18
  (27 shorter events, 0.4 us)
Async XLA Ops:
  6.5 221.2 %copy-start = (bf16[1,256,512]{2,1,0:T(8,128)(2,1)S(1)}, bf16[1,256,512]{2,1,0:T(8,128)(2,1)}, u32[]{:S(2)}) copy-start(bf16[1,256,512]{2,1,0:T(8,128)(2,1)} %param.15) | copy-start | bytes 786436
  6.5 94.5 %all-gather.6.cloned.1.call-start = ((), (), s32[]{:S(2)}) async-start(), calls=%async_computation.1 | async-start | bytes 4259840 | tf_op jit(solution)/shard_map/all_gather | solution.py:78
  7.3 193.4 %all-gather.12.cloned.1.call-start = ((), (), s32[]{:S(2)}) async-start(), calls=%async_computation.4 | async-start | bytes 9437184 | tf_op jit(solution)/shard_map/all_gather | solution.py:81
  8.7 97.1 %copy-start.4 = (s32[128,2]{0,1:T(2,128)S(1)}, s32[128,2]{0,1:T(2,128)}, u32[]{:S(2)}) copy-start(s32[128,2]{0,1:T(2,128)} %param.18) | copy-start | bytes 3076
  8.7 97.1 %copy-start.5 = (s32[128]{0:T(128)S(1)}, s32[128]{0:T(128)}, u32[]{:S(2)}) copy-start(s32[128]{0:T(128)} %param.19) | copy-start | bytes 1540
  8.7 97.6 %copy-start.1 = (bf16[512,512]{1,0:T(8,128)(2,1)S(1)}, bf16[512,512]{1,0:T(8,128)(2,1)}, u32[]{:S(2)}) copy-start(bf16[512,512]{1,0:T(8,128)(2,1)} %param.12) | copy-start | bytes 1572868
  200.7 4.9 %copy-start.2 = (f32[512]{0:T(512)S(1)}, f32[512]{0:T(512)}, u32[]{:S(2)}) copy-start(f32[512]{0:T(512)} %param.14) | copy-start | bytes 6148
  205.6 152.3 %copy-start.3 = (f32[4096]{0:T(1024)S(1)}, f32[4096]{0:T(1024)}, u32[]{:S(2)}) copy-start(f32[4096]{0:T(1024)} %param.20) | copy-start | bytes 49156
  206.6 20.8 %all-to-all-start = ((bf16[64,2,512]{2,1,0:T(2,128)(2,1)}), bf16[64,2,512]{2,1,0:T(2,128)(2,1)S(1)}, u32[]{:S(2)}, u32[]{:S(2)}) async-start(bf16[64,2,512]{2,1,0:T(2,128)(2,1)} %reshape.199), calls=%async_computation | async-start | bytes 262144 | tf_op jit(solution)/shard_map/all_to_all | solution.py:103
  217.0 53.0 %all-gather.8.cloned.1.call-start = ((), (), s32[]{:S(2)}) async-start(), calls=%async_computation.2 | async-start | bytes 3538944 | tf_op jit(solution)/shard_map/all_gather | solution.py:135
  228.8 129.1 %all-gather.10.cloned.1.call-start = ((), (), s32[]{:S(2)}) async-start(), calls=%async_computation.3 | async-start | bytes 6389760 | tf_op jit(solution)/shard_map/all_gather | solution.py:139
Sparse Core Ops, SparseCore 0:
  10.7 90.2 all-gather.5
  105.9 94.7 all-gather.11
  228.9 41.0 all-gather.7
  273.2 84.7 all-gather.9
